TPU v7x, 32 devices: a whole 2x2x4 slice. The times are simulated.
32 devices in a mesh: mem: 4 (over z), tile: 8 (over y, x, core).
Axes of the slice: x: 2, y: 2, z: 4, core: 2. Of those that a mesh axis runs over, the one named last changes fastest.
Arguments:
- source_blocks: bfloat16 [1024, 8, 2, 256], P('tile', 'mem'), may hold values from -6 to 6
- send_blocks: int32 [8, 8, 24], P('tile'), may hold values from 0 to 127
- recv_slot: int32 [8, 8, 24], P('tile'), may hold values from 0 to 95
- recv_weight: float32 [8, 8, 24], P('tile'), may hold values from 0.25 to 2
- recv_count: int32 [8, 8], P('tile'), may hold values from 0 to 24, as said below
- regional: bfloat16 [8, 2, 512, 384], P('mem', None, 'tile'), may hold values from -6 to 6
- x_operator: bfloat16 [512, 512], P(('mem', 'tile'))
- y_operator: bfloat16 [384, 384], P(('mem', 'tile'))
Outputs:
- blended: bfloat16 [8, 2, 512, 384], P('mem', None, 'tile')
Inputs may be any that keep to these rules, and one draw needn't show every extreme that they name: `recv_count`: live entries of one pair of tiles number at most 24; some pairs in every draw have 24.
All inputs are finite; a program needn't handle non-finite values.
Results may differ from a plain program's by a relative error of at most 0.0055.
Values may be sent and summed in bfloat16 or wider, within the bound.
No kernel may reach another device: no remote copies, remote signals or barrier semaphores. Data moves between devices by JAX's collectives and lax.ppermute only.
A program may use at most 128 MiB of HBM per device.

v0:
```python
import math
import jax
import jax.numpy as jnp
from jax import lax
from jax.sharding import PartitionSpec as P


def body(
    source_blocks, send_blocks, recv_slot, recv_weight, recv_count, regional, x_operator, y_operator
):
    tile_count = lax.axis_size("tile")
    member_count, level_count, columns, y_cells = regional.shape
    capacity = send_blocks.shape[2]
    block_cells = source_blocks.shape[3]
    block_side = math.isqrt(block_cells)
    picked = send_blocks[0].reshape(-1)
    packed = jnp.take(source_blocks, picked, axis=0).reshape(
        tile_count, capacity, member_count, level_count, block_cells
    )
    arrived = lax.all_to_all(packed, "tile", split_axis=0, concat_axis=0, tiled=True)
    slot_count = columns // block_side * (y_cells // block_side)
    live_mask = lax.broadcasted_iota(jnp.int32, (tile_count, capacity), 1) < recv_count[0][:, None]
    weights = jnp.where(live_mask, recv_weight[0], 0.0).reshape(-1)
    slot_match = recv_slot[0].reshape(-1)[None, :] == lax.broadcasted_iota(
        jnp.int32, (slot_count, tile_count * capacity), 0
    )
    remap_weights = jnp.where(slot_match, weights[None, :], 0.0).astype(jnp.bfloat16)
    remapped = jnp.dot(
        remap_weights,
        arrived.reshape(tile_count * capacity, -1),
        preferred_element_type=jnp.float32,
    )
    remapped = remapped.reshape(
        columns // block_side,
        y_cells // block_side,
        member_count,
        level_count,
        block_side,
        block_side,
    )
    remapped = remapped.transpose(2, 3, 0, 4, 1, 5).reshape(
        member_count, level_count, columns, y_cells
    )
    difference = (remapped - regional.astype(jnp.float32)).astype(jnp.bfloat16)
    x_lines = lax.all_to_all(difference, "tile", split_axis=3, concat_axis=2, tiled=True)
    after_first = jnp.einsum(
        "ax,mlxy->mlay",
        lax.all_gather(x_operator, ("mem", "tile"), axis=0, tiled=True),
        x_lines,
        preferred_element_type=jnp.float32,
    ).astype(jnp.bfloat16)
    tile_back = lax.all_to_all(after_first, "tile", split_axis=2, concat_axis=3, tiled=True)
    after_second = jnp.einsum(
        "by,mlxy->mlxb",
        lax.all_gather(y_operator, ("mem", "tile"), axis=0, tiled=True),
        tile_back,
        preferred_element_type=jnp.float32,
    )
    return (regional.astype(jnp.float32) + after_second).astype(jnp.bfloat16)


def solution(mesh):
    placed = (
        P("tile", "mem", None, None),
        P("tile", None, None),
        P("tile", None, None),
        P("tile", None, None),
        P("tile", None),
        P("mem", None, "tile", None),
        P(("mem", "tile"), None),
        P(("mem", "tile"), None),
    )
    return jax.shard_map(
        body, mesh=mesh, in_specs=placed, out_specs=P("mem", None, "tile", None), check_vma=False
    )
```

profile of v0, /device:TPU:0, one launch (start us, length us, event | category | flops | bytes accessed | tf_op | source)
XLA Modules:
  0.0 121.7 jit_solution(16398745087015653898)
XLA Ops:
  0.0 0.8 reshape_squeeze.6
  0.8 0.7 compare_and_fusion
  1.5 1.4 %gather_fusion = bf16[192,2,2,256]{3,2,1,0:T(2,128)(2,1)S(1)} fusion(bf16[128,2,2,256]{3,2,1,0:T(2,128)(2,1)S(1)} %copy-done, s32[1024]{0:T(1024)S(1)} %pad_clamp_fusion), kind=kCustom, calls=%fused_computation | custom fusion | bytes 787200 | tf_op jit(solution)/shard_map/jit(_take)/gather | solution.py:17
  3.0 1.2 broadcast_select_fusion
  4.2 5.2 %all-to-all-start = ((bf16[8,24,2,2,256]{4,3,2,1,0:T(2,128)(2,1)}), bf16[8,24,2,2,256]{4,3,2,1,0:T(2,128)(2,1)S(1)}, u32[]{:S(2)}, u32[]{:S(2)}) async-start(bf16[8,24,2,2,256]{4,3,2,1,0:T(2,128)(2,1)} %broadcast_select_fusion), calls=%async_computation | async-start | bytes 786432 | tf_op jit(solution)/shard_map/all_to_all | solution.py:20
  9.7 8.0 %all-to-all-done = bf16[8,24,2,2,256]{4,3,2,1,0:T(2,128)(2,1)S(1)} async-done(((bf16[8,24,2,2,256]{4,3,2,1,0:T(2,128)(2,1)}), bf16[8,24,2,2,256]{4,3,2,1,0:T(2,128)(2,1)S(1)}, u32[]{:S(2)}, u32[]{:S(2)}) %all-to-all-start) | async-done | bytes 393248 | tf_op jit(solution)/shard_map/all_to_all | solution.py:20
  18.2 1.9 %convolution_bitcast_fusion = f32[2,2,4,16,24,16]{4,5,3,1,0,2:T(8,128)} fusion(bf16[2,2,16,16,192,1]{4,3,2,1,0,5:T(8,128)(2,1)S(1)} %bitcast.53, bf16[192]{0:T(256)(128)(2,1)S(1)} %broadcast_select_fusion.1, s32[4,24]{1,0:T(4,128)S(1)} %multiply_add_fusion, s32[192]{0:T(256)S(1)} %eq.15), kind=kOutput, calls=%fused_computation.1 | convolution fusion | flops 37785600 | bytes 787968 | tf_op jit(solution)/shard_map/dot_general | solution.py:28
  20.0 2.2 %copy.17 = f32[2,2,4,16,24,16]{5,4,3,2,1,0:T(8,128)S(1)} copy(f32[2,2,4,16,24,16]{4,5,3,1,0,2:T(8,128)} %convolution_bitcast_fusion) | data formatting | bytes 786432 | tf_op jit(solution)/shard_map/transpose | solution.py:41
  22.3 1.6 %reshape.93 = f32[2,2,64,384]{3,2,1,0:T(8,128)} reshape(f32[2,2,4,16,24,16]{5,4,3,2,1,0:T(8,128)S(1)} %copy.17) | data formatting | bytes 786432 | tf_op jit(solution)/shard_map/reshape | solution.py:41
  23.9 1.1 fusion.3
  25.0 0.6 copy.18
  25.6 1.0 reshape.109
  26.6 3.4 %all-to-all-start.1 = ((bf16[8,2,6144]{2,1,0:T(2,128)(2,1)}), bf16[8,2,6144]{2,1,0:T(2,128)(2,1)S(1)}, u32[]{:S(2)}, u32[]{:S(2)}) async-start(bf16[8,2,6144]{2,1,0:T(2,128)(2,1)} %reshape.109), calls=%async_computation.1 | async-start | bytes 393216 | tf_op jit(solution)/shard_map/all_to_all | solution.py:45
  30.0 43.6 %all_gather.6 = bf16[512,512]{1,0:T(8,128)(2,1)S(1)} all-gather(bf16[16,512]{1,0:T(8,128)(2,1)S(1)} %copy-done.2), channel_id=1, replica_groups=mesh['mem'=4,'tile'=8] {'mem','tile'}, dimensions={0}, use_global_device_ids=true | all-gather | bytes 540672 | tf_op jit(solution)/shard_map/all_gather | solution.py:48
  73.6 0.3 reshape.110
  74.4 0.3 fusion.1
  74.8 0.4 copy.21
  75.2 1.4 %reshape.111 = bf16[8,2,6144]{2,1,0:T(2,128)(2,1)} reshape(bf16[512,2,2,48]{3,2,1,0:T(2,128)(2,1)S(1)} %bitcast.54) | data formatting | bytes 393216
  76.6 3.5 %all-to-all-start.2 = ((bf16[8,2,6144]{2,1,0:T(2,128)(2,1)}), bf16[8,2,6144]{2,1,0:T(2,128)(2,1)S(1)}, u32[]{:S(2)}, u32[]{:S(2)}) async-start(bf16[8,2,6144]{2,1,0:T(2,128)(2,1)} %reshape.111), calls=%async_computation.2 | async-start | bytes 393216 | tf_op jit(solution)/shard_map/all_to_all | solution.py:52
  80.1 39.3 %all-gather = bf16[32,12,384]{2,1,0:T(8,128)(2,1)S(1)} all-gather(bf16[1,12,384]{2,1,0:T(8,128)(2,1)S(1)} %bitcast.62), channel_id=1, replica_groups=mesh['mem'=4,'tile'=8] {'mem','tile'}, dimensions={0}, use_global_device_ids=true | all-gather | bytes 304128 | tf_op jit(solution)/shard_map/all_gather | solution.py:55
  119.5 0.5 reshape.112
  120.0 0.3 copy.30
  120.4 0.4 all_to_all.37
  120.8 1.0 fusion
  (29 shorter events, 1.4 us)
Async XLA Ops:
  0.0 1.5 %copy-start = (bf16[128,2,2,256]{3,2,1,0:T(2,128)(2,1)S(1)}, bf16[128,2,2,256]{3,2,1,0:T(2,128)(2,1)}, u32[]{:S(2)}) copy-start(bf16[128,2,2,256]{3,2,1,0:T(2,128)(2,1)} %param.8) | copy-start | bytes 786436
  0.0 9.4 %copy-start.6 = (s32[1,8]{1,0:T(1,128)S(1)}, s32[1,8]{1,0:T(1,128)}, u32[]{:S(2)}) copy-start(s32[1,8]{1,0:T(1,128)} %param.12) | copy-start | bytes 100
  0.0 9.5 %copy-start.5 = (f32[1,8,24]{2,1,0:T(8,128)S(1)}, f32[1,8,24]{2,1,0:T(8,128)}, u32[]{:S(2)}) copy-start(f32[1,8,24]{2,1,0:T(8,128)} %param.11) | copy-start | bytes 2308
  0.0 9.6 %copy-start.4 = (s32[1,8,24]{2,1,0:T(8,128)S(1)}, s32[1,8,24]{2,1,0:T(8,128)}, u32[]{:S(2)}) copy-start(s32[1,8,24]{2,1,0:T(8,128)} %param.10) | copy-start | bytes 2308
  4.2 13.5 %all-to-all-start = ((bf16[8,24,2,2,256]{4,3,2,1,0:T(2,128)(2,1)}), bf16[8,24,2,2,256]{4,3,2,1,0:T(2,128)(2,1)S(1)}, u32[]{:S(2)}, u32[]{:S(2)}) async-start(bf16[8,24,2,2,256]{4,3,2,1,0:T(2,128)(2,1)} %broadcast_select_fusion), calls=%async_computation | async-start | bytes 786432 | tf_op jit(solution)/shard_map/all_to_all | solution.py:20
  22.3 7.7 %copy-start.2 = (bf16[16,512]{1,0:T(8,128)(2,1)S(1)}, bf16[16,512]{1,0:T(8,128)(2,1)}, u32[]{:S(2)}) copy-start(bf16[16,512]{1,0:T(8,128)(2,1)} %param.14) | copy-start | bytes 49156
  26.6 47.0 %all-to-all-start.1 = ((bf16[8,2,6144]{2,1,0:T(2,128)(2,1)}), bf16[8,2,6144]{2,1,0:T(2,128)(2,1)S(1)}, u32[]{:S(2)}, u32[]{:S(2)}) async-start(bf16[8,2,6144]{2,1,0:T(2,128)(2,1)} %reshape.109), calls=%async_computation.1 | async-start | bytes 393216 | tf_op jit(solution)/shard_map/all_to_all | solution.py:45
  73.9 6.2 %copy-start.3 = (bf16[12,384]{1,0:T(8,128)(2,1)S(1)}, bf16[12,384]{1,0:T(8,128)(2,1)}, u32[]{:S(2)}) copy-start(bf16[12,384]{1,0:T(8,128)(2,1)} %param.15) | copy-start | bytes 27652
  76.6 44.2 %copy-start.1 = (bf16[2,2,64,384]{3,2,1,0:T(8,128)(2,1)S(1)}, bf16[2,2,64,384]{3,2,1,0:T(8,128)(2,1)}, u32[]{:S(2)}) copy-start(bf16[2,2,64,384]{3,2,1,0:T(8,128)(2,1)} %param.13) | copy-start | bytes 589828
  76.6 42.9 %all-to-all-start.2 = ((bf16[8,2,6144]{2,1,0:T(2,128)(2,1)}), bf16[8,2,6144]{2,1,0:T(2,128)(2,1)S(1)}, u32[]{:S(2)}, u32[]{:S(2)}) async-start(bf16[8,2,6144]{2,1,0:T(2,128)(2,1)} %reshape.111), calls=%async_computation.2 | async-start | bytes 393216 | tf_op jit(solution)/shard_map/all_to_all | solution.py:52
where the time goes:
time: 122 us
  blocking collectives  82.9 us (68%)
  local copies, waits for them, and re-layouts  12.4 us (10%)
  starting transfers between devices  12.1 us (10%)
  waiting for transfers between devices  7.98 us (7%)
  matrix products  3.14 us (3%)
  other arithmetic  3.08 us (3%)
    all_gather x1, blocking collectives, body(): lax.all_gather(x_operator, ('mem', 'tile'), axis=0, tiled=True)  43.6 us
    all_gather x1, blocking collectives, body(): lax.all_gather(y_operator, ('mem', 'tile'), axis=0, tiled=True)  39.3 us
    all_to_all x1, waiting for transfers between devices, body(): lax.all_to_all(packed, 'tile', split_axis=0, concat_axis=0, tiled=True)  7.98 us
    all_to_all x1, starting transfers between devices, body(): lax.all_to_all(packed, 'tile', split_axis=0, concat_axis=0, tiled=True)  5.18 us
    all_to_all x1, starting transfers between devices, body(): lax.all_to_all(after_first, 'tile', split_axis=2, concat_axis=3, tiled=True)  3.52 us
    all_to_all x1, starting transfers between devices, body(): lax.all_to_all(difference, 'tile', split_axis=3, concat_axis=2, tiled=True)  3.39 us
    unnamed x19, local copies, waits for them, and re-layouts  3.32 us
  transfers between devices with their start and end apart: 3, of which 1 were waited for; matrix products, arithmetic and copies ran while one was open for 0% of the time, Pallas kernels for 0%

commit v1 on v0

--- a/solution.py
+++ b/solution.py
@@ -3,6 +3,18 @@
 import jax.numpy as jnp
 from jax import lax
 from jax.sharding import PartitionSpec as P
+
+
+def gather_by_bits(x, axis, dim):
+    ways, here, lap = (lax.axis_size(axis), lax.axis_index(axis), x.shape[dim])
+    line, have = (x, 1)
+    while have < ways:
+        line = jnp.concatenate(
+            [line, lax.ppermute(line, axis, [(d, (d - have) % ways) for d in range(ways)])],
+            axis=dim,
+        )
+        have = 2 * have
+    return jnp.roll(line, here * lap, axis=dim)
 
 
 def body(
@@ -52,7 +64,7 @@
     tile_back = lax.all_to_all(after_first, "tile", split_axis=2, concat_axis=3, tiled=True)
     after_second = jnp.einsum(
         "by,mlxy->mlxb",
-        lax.all_gather(y_operator, ("mem", "tile"), axis=0, tiled=True),
+        gather_by_bits(y_operator, ("mem", "tile"), 0),
         tile_back,
         preferred_element_type=jnp.float32,
     )

time: 122 us -> 99.4 us (0.81)
  blocking collectives: 82.9 us -> 40.4 us
  starting transfers between devices: 12.1 us -> 26.2 us
  waiting for transfers between devices: 7.98 us -> 12.7 us
    all_gather x1 -> x0, blocking collectives: 39.3 us -> none  [body(): lax.all_gather(y_operator, ('mem', 'tile'), axis=0, tiled=True)]
    ppermute x0 -> x5, waiting for transfers between devices: none -> 12.7 us  [gather_by_bits(): lax.ppermute(line, axis, [(d, (d - have) % ways) for d in range(ways)])]
    ppermute x0 -> x5, starting transfers between devices: none -> 11.3 us  [gather_by_bits(): lax.ppermute(line, axis, [(d, (d - have) % ways) for d in range(ways)])]
    all_to_all x1, waiting for transfers between devices: 7.98 us -> 0.01 us  [body(): lax.all_to_all(packed, 'tile', split_axis=0, concat_axis=0, tiled=True)]
    all_gather x1, blocking collectives: 43.6 us -> 40.4 us  [body(): lax.all_gather(x_operator, ('mem', 'tile'), axis=0, tiled=True)]
    all_to_all x1, starting transfers between devices: 3.39 us -> 6.34 us  [body(): lax.all_to_all(difference, 'tile', split_axis=3, concat_axis=2, tiled=True)]
    unnamed x19 -> x18, local copies, waits for them, and re-layouts: 3.32 us -> 3.25 us
  transfers between devices with their start and end apart: 3 -> 8, of which waited for: 1 -> 3; matrix products, arithmetic and copies ran while one was open for 0% -> 13% of each run, Pallas kernels for 0% -> 0%
where the time goes in v1:
time: 99.4 us; the launch traced here: 98.9 us
  blocking collectives  40.4 us (41%)
  starting transfers between devices  26.2 us (26%)
  local copies, waits for them, and re-layouts  13.1 us (13%)
  waiting for transfers between devices  12.7 us (13%)
  matrix products  3.18 us (3%)
  other arithmetic  3.13 us (3%)
    all_gather x1, blocking collectives, body(): lax.all_gather(x_operator, ('mem', 'tile'), axis=0, tiled=True)  40.4 us
    ppermute x5, waiting for transfers between devices, gather_by_bits(): lax.ppermute(line, axis, [(d, (d - have) % ways) for d in range(ways)])  12.7 us
    ppermute x5, starting transfers between devices, gather_by_bits(): lax.ppermute(line, axis, [(d, (d - have) % ways) for d in range(ways)])  11.3 us
    all_to_all x1, starting transfers between devices, body(): lax.all_to_all(difference, 'tile', split_axis=3, concat_axis=2, tiled=True)  6.34 us
    all_to_all x1, starting transfers between devices, body(): lax.all_to_all(packed, 'tile', split_axis=0, concat_axis=0, tiled=True)  5.18 us
    all_to_all x1, starting transfers between devices, body(): lax.all_to_all(after_first, 'tile', split_axis=2, concat_axis=3, tiled=True)  3.39 us
    unnamed x18, local copies, waits for them, and re-layouts  3.25 us
    transpose x1, local copies, waits for them, and re-layouts, body(): remapped.transpose(2, 3, 0, 4, 1, 5)  2.25 us
  transfers between devices with their start and end apart: 8, of which 3 were waited for; matrix products, arithmetic and copies ran while one was open for 13% of the time, Pallas kernels for 0%

profile of v1, /device:TPU:0, one launch (start us, length us, event | category | flops | bytes accessed | tf_op | source)
XLA Modules:
  0.0 98.9 jit_solution(18323613092247643148)
XLA Ops:
  0.0 0.8 reshape_squeeze.6
  0.8 0.7 compare_and_fusion
  1.5 1.4 %gather_fusion = bf16[192,2,2,256]{3,2,1,0:T(2,128)(2,1)S(1)} fusion(bf16[128,2,2,256]{3,2,1,0:T(2,128)(2,1)S(1)} %copy-done, s32[1024]{0:T(1024)S(1)} %pad_clamp_fusion), kind=kCustom, calls=%fused_computation | custom fusion | bytes 787200 | tf_op jit(solution)/shard_map/jit(_take)/gather | solution.py:29
  3.0 1.2 %broadcast_select_fusion = bf16[8,24,2,2,256]{4,3,2,1,0:T(2,128)(2,1)} fusion(bf16[8,24,2,2,256]{4,3,2,1,0:T(2,128)(2,1)S(1)} %bitcast.58, pred[8,24]{1,0:T(8,128)(4,1)S(1)} %compare_and_fusion), kind=kLoop, calls=%fused_computation.6 | loop fusion | flops 196608 | bytes 786624 | tf_op jit(solution)/shard_map/jit(_take)/select_n | solution.py:29
  4.2 5.2 %all-to-all-start = ((bf16[8,24,2,2,256]{4,3,2,1,0:T(2,128)(2,1)}), bf16[8,24,2,2,256]{4,3,2,1,0:T(2,128)(2,1)S(1)}, u32[]{:S(2)}, u32[]{:S(2)}) async-start(bf16[8,24,2,2,256]{4,3,2,1,0:T(2,128)(2,1)} %broadcast_select_fusion), calls=%async_computation | async-start | bytes 786432 | tf_op jit(solution)/shard_map/all_to_all | solution.py:32
  9.4 5.7 %collective-permute-start = (bf16[12,384]{1,0:T(8,128)(2,1)S(1)}, bf16[12,384]{1,0:T(8,128)(2,1)S(1)}, u32[]{:S(2)}, u32[]{:S(2)}) collective-permute-start(bf16[12,384]{1,0:T(8,128)(2,1)S(1)} %copy-done.2), channel_id=1, source_target_pairs={{0,31},{1,0},{2,1},{3,2},{4,3},{5,4},{6,5},{7,6},{8,7},{9,8},{10,9... | collective-permute-start | bytes 27656 | tf_op jit(solution)/shard_map/ppermute | solution.py:13
  15.4 1.1 %collective-permute-done = bf16[12,384]{1,0:T(8,128)(2,1)S(1)} collective-permute-done((bf16[12,384]{1,0:T(8,128)(2,1)S(1)}, bf16[12,384]{1,0:T(8,128)(2,1)S(1)}, u32[]{:S(2)}, u32[]{:S(2)}) %collective-permute-start) | collective-permute-done | bytes 9248 | tf_op jit(solution)/shard_map/ppermute | solution.py:13
  16.5 4.0 %collective-permute-start.1 = (bf16[24,384]{1,0:T(8,128)(2,1)S(1)}, bf16[24,384]{1,0:T(8,128)(2,1)S(1)}, u32[]{:S(2)}, u32[]{:S(2)}) collective-permute-start(bf16[24,384]{1,0:T(8,128)(2,1)S(1)} %pad_maximum_fusion.2), channel_id=1, source_target_pairs={{0,30},{1,31},{2,0},{3,1},{4,2},{5,3},{6,4},{7,5},{8,6},{9,7},{10,... | collective-permute-start | bytes 55304 | tf_op jit(solution)/shard_map/ppermute | solution.py:13
  20.6 1.4 %collective-permute-done.1 = bf16[24,384]{1,0:T(8,128)(2,1)S(1)} collective-permute-done((bf16[24,384]{1,0:T(8,128)(2,1)S(1)}, bf16[24,384]{1,0:T(8,128)(2,1)S(1)}, u32[]{:S(2)}, u32[]{:S(2)}) %collective-permute-start.1) | collective-permute-done | bytes 18464 | tf_op jit(solution)/shard_map/ppermute | solution.py:13
  22.0 1.5 %collective-permute-start.2 = (bf16[48,384]{1,0:T(8,128)(2,1)S(1)}, bf16[48,384]{1,0:T(8,128)(2,1)S(1)}, u32[]{:S(2)}, u32[]{:S(2)}) collective-permute-start(bf16[48,384]{1,0:T(8,128)(2,1)S(1)} %pad_maximum_fusion.1), channel_id=1, source_target_pairs={{0,28},{1,29},{2,30},{3,31},{4,0},{5,1},{6,2},{7,3},{8,4},{9,5},{1... | collective-permute-start | bytes 110600 | tf_op jit(solution)/shard_map/ppermute | solution.py:13
  23.9 1.9 %convolution_bitcast_fusion = f32[2,2,4,16,24,16]{4,5,3,1,0,2:T(8,128)} fusion(bf16[2,2,16,16,192,1]{4,3,2,1,0,5:T(8,128)(2,1)S(1)} %bitcast.54, bf16[192]{0:T(256)(128)(2,1)S(1)} %broadcast_select_fusion.1, s32[4,24]{1,0:T(4,128)S(1)} %multiply_add_fusion, s32[192]{0:T(256)S(1)} %eq.18), kind=kOutput, calls=%fused_computation.1 | convolution fusion | flops 37785600 | bytes 787968 | tf_op jit(solution)/shard_map/dot_general | solution.py:40
  25.8 2.2 %copy.17 = f32[2,2,4,16,24,16]{5,4,3,2,1,0:T(8,128)S(1)} copy(f32[2,2,4,16,24,16]{4,5,3,1,0,2:T(8,128)} %convolution_bitcast_fusion) | data formatting | bytes 786432 | tf_op jit(solution)/shard_map/transpose | solution.py:53
  28.0 1.6 %reshape.93 = f32[2,2,64,384]{3,2,1,0:T(8,128)} reshape(f32[2,2,4,16,24,16]{5,4,3,2,1,0:T(8,128)S(1)} %copy.17) | data formatting | bytes 786432 | tf_op jit(solution)/shard_map/reshape | solution.py:53
  29.7 1.1 %fusion.3 = bf16[2,2,64,384]{3,2,1,0:T(8,128)(2,1)S(1)} fusion(f32[2,2,64,384]{3,2,1,0:T(8,128)} %reshape.93, bf16[2,2,64,384]{3,2,1,0:T(8,128)(2,1)} %param.13), kind=kLoop, calls=%fused_computation.10 | loop fusion | flops 294912 | bytes 786432 | tf_op jit(solution)/shard_map/convert_element_type | solution.py:56
  30.8 0.6 copy.18
  31.4 1.0 reshape.106
  32.4 6.3 %all-to-all-start.1 = ((bf16[8,2,6144]{2,1,0:T(2,128)(2,1)}), bf16[8,2,6144]{2,1,0:T(2,128)(2,1)S(1)}, u32[]{:S(2)}, u32[]{:S(2)}) async-start(bf16[8,2,6144]{2,1,0:T(2,128)(2,1)} %reshape.106), calls=%async_computation.1 | async-start | bytes 393216 | tf_op jit(solution)/shard_map/all_to_all | solution.py:57
  38.7 40.4 %all_gather.3 = bf16[512,512]{1,0:T(8,128)(2,1)S(1)} all-gather(bf16[16,512]{1,0:T(8,128)(2,1)S(1)} %copy-done.3), channel_id=1, replica_groups=mesh['mem'=4,'tile'=8] {'mem','tile'}, dimensions={0}, use_global_device_ids=true | all-gather | bytes 540672 | tf_op jit(solution)/shard_map/all_gather | solution.py:60
  80.8 1.4 %reshape.108 = bf16[8,2,6144]{2,1,0:T(2,128)(2,1)} reshape(bf16[512,2,2,48]{3,2,1,0:T(2,128)(2,1)S(1)} %bitcast.55) | data formatting | bytes 393216
  82.2 3.4 %all-to-all-start.2 = ((bf16[8,2,6144]{2,1,0:T(2,128)(2,1)}), bf16[8,2,6144]{2,1,0:T(2,128)(2,1)S(1)}, u32[]{:S(2)}, u32[]{:S(2)}) async-start(bf16[8,2,6144]{2,1,0:T(2,128)(2,1)} %reshape.108), calls=%async_computation.2 | async-start | bytes 393216 | tf_op jit(solution)/shard_map/all_to_all | solution.py:64
  85.9 10.2 %collective-permute-done.4 = bf16[192,384]{1,0:T(8,128)(2,1)S(1)} collective-permute-done((bf16[192,384]{1,0:T(8,128)(2,1)S(1)}, bf16[192,384]{1,0:T(8,128)(2,1)S(1)}, u32[]{:S(2)}, u32[]{:S(2)}) %collective-permute-start.4) | collective-permute-done | bytes 147488 | tf_op jit(solution)/shard_map/ppermute | solution.py:13
  96.1 0.6 concatenate.26
  96.7 0.5 reshape.109
  97.9 1.0 fusion
  (42 shorter events, 3.5 us)
Async XLA Ops:
  0.0 1.5 %copy-start = (bf16[128,2,2,256]{3,2,1,0:T(2,128)(2,1)S(1)}, bf16[128,2,2,256]{3,2,1,0:T(2,128)(2,1)}, u32[]{:S(2)}) copy-start(bf16[128,2,2,256]{3,2,1,0:T(2,128)(2,1)} %param.8) | copy-start | bytes 786436
  0.0 9.4 %copy-start.2 = (bf16[12,384]{1,0:T(8,128)(2,1)S(1)}, bf16[12,384]{1,0:T(8,128)(2,1)}, u32[]{:S(2)}) copy-start(bf16[12,384]{1,0:T(8,128)(2,1)} %param.15) | copy-start | bytes 27652
  0.0 15.1 %copy-start.6 = (s32[1,8]{1,0:T(1,128)S(1)}, s32[1,8]{1,0:T(1,128)}, u32[]{:S(2)}) copy-start(s32[1,8]{1,0:T(1,128)} %param.12) | copy-start | bytes 100
  0.0 15.3 %copy-start.5 = (f32[1,8,24]{2,1,0:T(8,128)S(1)}, f32[1,8,24]{2,1,0:T(8,128)}, u32[]{:S(2)}) copy-start(f32[1,8,24]{2,1,0:T(8,128)} %param.11) | copy-start | bytes 2308
  0.0 20.5 %copy-start.4 = (s32[1,8,24]{2,1,0:T(8,128)S(1)}, s32[1,8,24]{2,1,0:T(8,128)}, u32[]{:S(2)}) copy-start(s32[1,8,24]{2,1,0:T(8,128)} %param.10) | copy-start | bytes 2308
  4.2 19.2 %all-to-all-start = ((bf16[8,24,2,2,256]{4,3,2,1,0:T(2,128)(2,1)}), bf16[8,24,2,2,256]{4,3,2,1,0:T(2,128)(2,1)S(1)}, u32[]{:S(2)}, u32[]{:S(2)}) async-start(bf16[8,24,2,2,256]{4,3,2,1,0:T(2,128)(2,1)} %broadcast_select_fusion), calls=%async_computation | async-start | bytes 786432 | tf_op jit(solution)/shard_map/all_to_all | solution.py:32
  9.4 7.1 %collective-permute-start = (bf16[12,384]{1,0:T(8,128)(2,1)S(1)}, bf16[12,384]{1,0:T(8,128)(2,1)S(1)}, u32[]{:S(2)}, u32[]{:S(2)}) collective-permute-start(bf16[12,384]{1,0:T(8,128)(2,1)S(1)} %copy-done.2), channel_id=1, source_target_pairs={{0,31},{1,0},{2,1},{3,2},{4,3},{5,4},{6,5},{7,6},{8,7},{9,8},{10,9... | collective-permute-start | bytes 27656 | tf_op jit(solution)/shard_map/ppermute | solution.py:13
  16.5 5.4 %collective-permute-start.1 = (bf16[24,384]{1,0:T(8,128)(2,1)S(1)}, bf16[24,384]{1,0:T(8,128)(2,1)S(1)}, u32[]{:S(2)}, u32[]{:S(2)}) collective-permute-start(bf16[24,384]{1,0:T(8,128)(2,1)S(1)} %pad_maximum_fusion.2), channel_id=1, source_target_pairs={{0,30},{1,31},{2,0},{3,1},{4,2},{5,3},{6,4},{7,5},{8,6},{9,7},{10,... | collective-permute-start | bytes 55304 | tf_op jit(solution)/shard_map/ppermute | solution.py:13
  22.0 57.1 %collective-permute-start.2 = (bf16[48,384]{1,0:T(8,128)(2,1)S(1)}, bf16[48,384]{1,0:T(8,128)(2,1)S(1)}, u32[]{:S(2)}, u32[]{:S(2)}) collective-permute-start(bf16[48,384]{1,0:T(8,128)(2,1)S(1)} %pad_maximum_fusion.1), channel_id=1, source_target_pairs={{0,28},{1,29},{2,30},{3,31},{4,0},{5,1},{6,2},{7,3},{8,4},{9,5},{1... | collective-permute-start | bytes 110600 | tf_op jit(solution)/shard_map/ppermute | solution.py:13
  28.0 10.7 %copy-start.3 = (bf16[16,512]{1,0:T(8,128)(2,1)S(1)}, bf16[16,512]{1,0:T(8,128)(2,1)}, u32[]{:S(2)}) copy-start(bf16[16,512]{1,0:T(8,128)(2,1)} %param.14) | copy-start | bytes 49156
  32.4 46.8 %all-to-all-start.1 = ((bf16[8,2,6144]{2,1,0:T(2,128)(2,1)}), bf16[8,2,6144]{2,1,0:T(2,128)(2,1)S(1)}, u32[]{:S(2)}, u32[]{:S(2)}) async-start(bf16[8,2,6144]{2,1,0:T(2,128)(2,1)} %reshape.106), calls=%async_computation.1 | async-start | bytes 393216 | tf_op jit(solution)/shard_map/all_to_all | solution.py:57
  79.1 6.5 %collective-permute-start.3 = (bf16[96,384]{1,0:T(8,128)(2,1)S(1)}, bf16[96,384]{1,0:T(8,128)(2,1)S(1)}, u32[]{:S(2)}, u32[]{:S(2)}) collective-permute-start(bf16[96,384]{1,0:T(8,128)(2,1)S(1)} %pad_maximum_fusion), channel_id=1, source_target_pairs={{0,24},{1,25},{2,26},{3,27},{4,28},{5,29},{6,30},{7,31},{8,0},{9,1... | collective-permute-start | bytes 221192 | tf_op jit(solution)/shard_map/ppermute | solution.py:13
  82.2 14.5 %all-to-all-start.2 = ((bf16[8,2,6144]{2,1,0:T(2,128)(2,1)}), bf16[8,2,6144]{2,1,0:T(2,128)(2,1)S(1)}, u32[]{:S(2)}, u32[]{:S(2)}) async-start(bf16[8,2,6144]{2,1,0:T(2,128)(2,1)} %reshape.108), calls=%async_computation.2 | async-start | bytes 393216 | tf_op jit(solution)/shard_map/all_to_all | solution.py:64
  85.6 12.3 %copy-start.1 = (bf16[2,2,64,384]{3,2,1,0:T(8,128)(2,1)S(1)}, bf16[2,2,64,384]{3,2,1,0:T(8,128)(2,1)}, u32[]{:S(2)}) copy-start(bf16[2,2,64,384]{3,2,1,0:T(8,128)(2,1)} %param.13) | copy-start | bytes 589828
  85.8 10.3 %collective-permute-start.4 = (bf16[192,384]{1,0:T(8,128)(2,1)S(1)}, bf16[192,384]{1,0:T(8,128)(2,1)S(1)}, u32[]{:S(2)}, u32[]{:S(2)}) collective-permute-start(bf16[192,384]{1,0:T(8,128)(2,1)S(1)} %concatenate.25), channel_id=1, source_target_pairs={{0,16},{1,17},{2,18},{3,19},{4,20},{5,21},{6,22},{7,23},{8,24},{9,... | collective-permute-start | bytes 442376 | tf_op jit(solution)/shard_map/ppermute | solution.py:13
